TPU v7x, 256 devices: a whole 4x4x8 slice. The times are simulated.
256 devices in a mesh: dp: 64 (over x, z_lo, y, core), fsdp: 4 (over z_hi).
Axes of the slice: x: 4, y: 4, z: 8 (z_hi: 4, z_lo: 2; z = z_hi * 2 + z_lo), core: 2. Of those that a mesh axis runs over, the one named last changes fastest.
Arguments:
- bag_ids: int32 [32768, 64, 4], P(('dp', 'fsdp')), may hold values from 0 to 8191
- bag_counts: int32 [32768, 64], P(('dp', 'fsdp')), may hold values from 1 to 4
- emb_table: bfloat16 [8192, 8192], P(None, 'dp'), may hold values from -3 to 3
- cross_down: bfloat16 [8192, 512], P('fsdp'), may hold values from -0.0625 to 0.0625
- cross_up: bfloat16 [512, 8192], P(None, 'fsdp'), may hold values from -0.25 to 0.25
- cross_bias: float32 [8192], replicated, may hold values from -2 to 2
- cotangent: bfloat16 [32768, 8192], P(('dp', 'fsdp')), may hold values from -4 to 4
Outputs:
- table_grad: float32 [8192, 8192], P('fsdp', 'dp')
Inputs may be any that keep to these rules, and one draw needn't show every extreme that they name: `bag_ids`: ids at positions at or past a bag's count are read by no step.
All inputs are finite; a program needn't handle non-finite values.
Results may differ from a plain program's by a relative error of at most 0.0045.
Values may be sent and summed in bfloat16 or wider, within the bound.
No kernel may reach another device: no remote copies, remote signals or barrier semaphores. Data moves between devices by JAX's collectives and lax.ppermute only.
A program may use at most 192 MiB of HBM per device.

v0:
```python
import jax
import jax.numpy as jnp
from jax import lax
from jax.sharding import PartitionSpec as P


def scatter_rows(height, index_rows, grads, table_count, slot_count, embed_width, offset):
    sample_count = index_rows.shape[0]
    local_rows = index_rows.reshape(sample_count, table_count, slot_count) - offset
    inside = (local_rows >= 0) & (local_rows < height)
    table_iota = lax.broadcasted_iota(jnp.int32, local_rows.shape, 1)
    flat_rows = jnp.where(inside, local_rows * table_count + table_iota, height * table_count)
    column_grads = grads.reshape(sample_count, table_count, 1, embed_width).astype(jnp.float32)
    updates = jnp.broadcast_to(column_grads, (sample_count, table_count, slot_count, embed_width))
    target = jnp.zeros((height * table_count, embed_width), jnp.float32)
    target = target.at[flat_rows.reshape(-1)].add(updates.reshape(-1, embed_width), mode="drop")
    return target


def on_device(bag_ids, bag_counts, emb_table, cross_down, cross_up, cross_bias, cotangent):
    row_count, table_count, slot_count = bag_ids.shape
    vocab_rows, col_piece = emb_table.shape
    dp_size = lax.axis_size("dp")
    local_tables = table_count // dp_size
    embed_width = col_piece // local_tables
    slot_iota = lax.broadcasted_iota(jnp.int32, bag_ids.shape, 2)
    live_ids = jnp.where(slot_iota < bag_counts[:, :, None], bag_ids, vocab_rows)
    send_ids = live_ids.reshape(row_count, table_count * slot_count)
    got_ids = lax.all_to_all(send_ids, "dp", split_axis=1, concat_axis=0, tiled=True)
    sample_count = got_ids.shape[0]
    table_iota = lax.broadcasted_iota(jnp.int32, (sample_count, local_tables, slot_count), 1)
    flat_ids = got_ids.reshape(sample_count, local_tables, slot_count) * local_tables + table_iota
    picked = jnp.take(emb_table, flat_ids, axis=0, mode="fill", fill_value=0)
    pooled_local = jnp.sum(picked.astype(jnp.float32), axis=2).astype(jnp.bfloat16)
    pooled_local = pooled_local.reshape(sample_count, col_piece)
    pooled = lax.all_to_all(pooled_local, "dp", split_axis=0, concat_axis=1, tiled=True)
    upstream = cotangent.astype(jnp.float32)
    grad_gate = (upstream * pooled.astype(jnp.float32)).astype(jnp.bfloat16)
    down_full, up_full = (
        lax.all_gather(cross_down, "fsdp", axis=0, tiled=True),
        lax.all_gather(cross_up, "fsdp", axis=1, tiled=True),
    )
    low_rank = jnp.dot(pooled, down_full, preferred_element_type=jnp.float32).astype(jnp.bfloat16)
    gate_value = jnp.dot(low_rank, up_full, preferred_element_type=jnp.float32) + cross_bias
    grad_low = lax.dot_general(
        grad_gate, up_full, (((1,), (1,)), ((), ())), preferred_element_type=jnp.float32
    ).astype(jnp.bfloat16)
    back_term = lax.dot_general(
        grad_low, down_full, (((1,), (1,)), ((), ())), preferred_element_type=jnp.float32
    )
    grad_pooled = (upstream * (gate_value + 1.0) + back_term).astype(jnp.bfloat16)
    grad_local = lax.all_to_all(grad_pooled, "dp", split_axis=1, concat_axis=0, tiled=True)
    partial_value = scatter_rows(
        vocab_rows, got_ids, grad_local, local_tables, slot_count, embed_width, 0
    )
    return lax.psum_scatter(partial_value, "fsdp", scatter_dimension=0, tiled=True)


def solution(mesh):
    placed = (
        P(("dp", "fsdp"), None, None),
        P(("dp", "fsdp"), None),
        P(None, "dp"),
        P("fsdp", None),
        P(None, "fsdp"),
        P(),
        P(("dp", "fsdp"), None),
    )
    return jax.shard_map(
        on_device, mesh=mesh, in_specs=placed, out_specs=P("fsdp", "dp"), check_vma=False
    )
```

profile of v0, /device:TPU:1, one launch (start us, length us, event | category | flops | bytes accessed | tf_op | source)
XLA Modules:
  0.0 684.6 jit_solution(626548155860651845)
XLA Ops:
  6.5 0.7 all-gather.3.cloned.1.call-update
  7.3 0.7 all-gather.5.cloned.1.call-update
  8.1 18.7 %all_to_all.45 = s32[128,64,4]{0,2,1:T(4,128)S(1)} all-to-all(s32[128,64,4]{0,2,1:T(4,128)S(1)} %fusion.24), channel_id=1, replica_groups=mesh['dp'=64,'fsdp'=4] {'dp'}, dimensions={1} | all-to-all | bytes 262144 | tf_op jit(solution)/shard_map/all_to_all | solution.py:29
  26.8 2.7 copy.10
  29.5 5.1 reshape.183
  34.6 1.7 copy.9
  36.4 114.2 %gather_fusion = bf16[32768,128]{1,0:T(8,128)(2,1)} fusion(bf16[8192,128]{1,0:T(8,128)(2,1)S(1)} %copy-done, s32[32768]{0:T(1024)S(1)} %broadcast_clamp_fusion), kind=kCustom, calls=%fused_computation | custom fusion | bytes 16908288 | tf_op jit(solution)/shard_map/jit(_take)/gather | solution.py:33
  150.6 47.3 %select_reduce_fusion = bf16[8192,128]{1,0:T(8,128)(2,1)} fusion(bf16[8192,1,4,128]{3,2,0,1:T(4,128)(2,1)} %bitcast.54, pred[8192,4]{1,0:T(8,128)(4,1)S(1)} %copy.9), kind=kLoop, calls=%fused_computation.7 | loop fusion | flops 7340032 | bytes 10518528 | tf_op jit(solution)/shard_map/reduce_sum | solution.py:34
  197.9 4.6 all-to-all-start.1
  202.5 2.7 copy.8
  205.1 6.1 reshape.176
  211.3 87.0 %all-to-all-done.1 = bf16[64,128,128]{2,1,0:T(8,128)(2,1)S(1)} async-done(((bf16[64,128,128]{2,1,0:T(8,128)(2,1)}), bf16[64,128,128]{2,1,0:T(8,128)(2,1)S(1)}, u32[]{:S(2)}, u32[]{:S(2)}) %all-to-all-start.1) | async-done | bytes 2097184 | tf_op jit(solution)/shard_map/all_to_all | solution.py:36
  298.3 48.7 %all-gather.5.cloned.1.call-done = bf16[512,8192]{1,0:T(8,128)(2,1)} async-done(((bf16[512,2048]{1,0:T(8,128)(2,1)}), bf16[512,8192]{1,0:T(8,128)(2,1)}) %all-gather.5.cloned.1.call-update) | async-done | bytes 8388624 | tf_op jit(solution)/shard_map/all_gather | solution.py:41
  347.0 11.1 %fusion.1 = f32[128,8192]{1,0:T(8,128)} fusion(bf16[512,8192]{1,0:T(8,128)(2,1)} %all-gather.5.cloned.1.call-done, bf16[128,8192]{1,0:T(8,128)(2,1)} %param.13, f32[8192]{0:T(1024)S(1)} %copy-done.3, bf16[8192,512]{1,0:T(8,128)(2,1)} %all-gather.3.cloned.1.call-done, bf16[64,128,128]{2,1,0:T(8,128)(2,1)S(1)} %all-to-all-done.1), kind=kOutput, calls=%fused_computation.5 | convolution fusion | flops 2151743488 | bytes 25198592 | tf_op jit(solution)/shard_map/dot_general | solution.py:44
  358.1 15.4 %fusion.13 = bf16[16,64,8,128]{3,2,1,0:T(8,128)(2,1)} fusion(f32[128,8192]{1,0:T(8,128)} %fusion.1, bf16[8192,512]{1,0:T(8,128)(2,1)} %all-gather.3.cloned.1.call-done, bf16[512,8192]{1,0:T(8,128)(2,1)} %all-gather.5.cloned.1.call-done, bf16[128,8192]{1,0:T(8,128)(2,1)} %param.13, bf16[64,128,128]{2,1,0:T(8,128)(2,1)S(1)} %all-to-all-done.1), kind=kOutput, calls=%fused_computation.19 | convolution fusion | flops 2153840640 | bytes 27262976 | tf_op jit(solution)/shard_map/dot_general | solution.py:48
  373.5 3.5 copy.32
  377.0 7.9 %all-to-all-start.2 = ((bf16[128,64,128]{2,0,1:T(8,128)(2,1)}), bf16[128,64,128]{2,0,1:T(8,128)(2,1)S(1)}, u32[]{:S(2)}, u32[]{:S(2)}) async-start(bf16[128,64,128]{2,0,1:T(8,128)(2,1)} %bitcast.57), calls=%async_computation.2 | async-start | bytes 4194304 | tf_op jit(solution)/shard_map/all_to_all | solution.py:52
  384.9 0.3 reduce-scatter.2.cloned.1.call-start
  385.2 0.2 compare_select_fusion
  385.4 28.5 %all-to-all-done.2 = bf16[128,64,128]{2,0,1:T(8,128)(2,1)S(1)} async-done(((bf16[128,64,128]{2,0,1:T(8,128)(2,1)}), bf16[128,64,128]{2,0,1:T(8,128)(2,1)S(1)}, u32[]{:S(2)}, u32[]{:S(2)}) %all-to-all-start.2) | async-done | bytes 2097184 | tf_op jit(solution)/shard_map/all_to_all | solution.py:52
  414.0 0.5 convert_element_type.44
  414.5 7.4 %broadcast_in_dim.31 = f32[8192,1,4,128]{3,2,0,1:T(4,128)} broadcast(f32[8192,128]{1,0:T(8,128)S(1)} %bitcast.56), dimensions={0,3} | broadcast | bytes 20971520 | tf_op jit(solution)/shard_map/broadcast_in_dim | solution.py:14
  421.9 176.5 %scatter_custom_fusion = f32[8192,128]{1,0:T(8,128)} fusion(s32[32768]{0:T(1024)S(1)} %bitcast.60, f32[32768,128]{1,0:T(8,128)} %bitcast.55, f32[]{:T(128)} %constant.7.clone.1), kind=kCustom, calls=%fused_computation.15 | custom fusion | flops 4194304 | bytes 4194816 | tf_op jit(solution)/shard_map/scatter-add | solution.py:16
  598.5 79.6 %reduce-scatter.2.cloned.1.call-done = f32[2048,128]{1,0:T(8,128)} async-done(((f32[8192,128]{1,0:T(8,128)}), f32[2048,128]{1,0:T(8,128)}) %reduce-scatter.2.cloned.1.call-update) | async-done | bytes 1048592 | tf_op jit(solution)/shard_map/reduce_scatter | solution.py:56
  (18 shorter events, 0.3 us)
Async XLA Ops:
  6.5 29.9 %copy-start = (bf16[8192,128]{1,0:T(8,128)(2,1)S(1)}, bf16[8192,128]{1,0:T(8,128)(2,1)}, u32[]{:S(2)}) copy-start(bf16[8192,128]{1,0:T(8,128)(2,1)} %param.9) | copy-start | bytes 6291460
  6.5 1.5 copy-start.2
  6.5 1.5 copy-start.4
  6.5 291.8 %all-gather.3.cloned.1.call-start = ((), (), s32[]{:S(2)}) async-start(), calls=%async_computation.4 | async-start | bytes 10485760 | tf_op jit(solution)/shard_map/all_gather | solution.py:40
  7.3 339.7 %all-gather.5.cloned.1.call-start = ((), (), s32[]{:S(2)}) async-start(), calls=%async_computation.5 | async-start | bytes 10485760 | tf_op jit(solution)/shard_map/all_gather | solution.py:41
  197.9 100.4 %all-to-all-start.1 = ((bf16[64,128,128]{2,1,0:T(8,128)(2,1)}), bf16[64,128,128]{2,1,0:T(8,128)(2,1)S(1)}, u32[]{:S(2)}, u32[]{:S(2)}) async-start(bf16[64,128,128]{2,1,0:T(8,128)(2,1)} %bitcast.58), calls=%async_computation.1 | async-start | bytes 4194304 | tf_op jit(solution)/shard_map/all_to_all | solution.py:36
  202.5 144.5 %copy-start.3 = (f32[8192]{0:T(1024)S(1)}, f32[8192]{0:T(1024)}, u32[]{:S(2)}) copy-start(f32[8192]{0:T(1024)} %param.12) | copy-start | bytes 98308
  377.0 37.0 %all-to-all-start.2 = ((bf16[128,64,128]{2,0,1:T(8,128)(2,1)}), bf16[128,64,128]{2,0,1:T(8,128)(2,1)S(1)}, u32[]{:S(2)}, u32[]{:S(2)}) async-start(bf16[128,64,128]{2,0,1:T(8,128)(2,1)} %bitcast.57), calls=%async_computation.2 | async-start | bytes 4194304 | tf_op jit(solution)/shard_map/all_to_all | solution.py:52
  384.9 293.1 %reduce-scatter.2.cloned.1.call-start = ((), (), s32[]{:S(2)}) async-start(), calls=%async_computation.6 | async-start | bytes 5242880 | tf_op jit(solution)/shard_map/reduce_scatter | solution.py:56
  421.9 256.1 %copy-start.1 = (bf16[8192,128]{1,0:T(8,128)(2,1)S(1)}, bf16[8192,128]{1,0:T(8,128)(2,1)}, u32[]{:S(2)}) copy-start(bf16[8192,128]{1,0:T(8,128)(2,1)} %param.9) | copy-start | bytes 6291460
Sparse Core Ops, SparseCore 0:
  9.2 159.0 all-gather.2
  170.1 176.8 all-gather.4
  598.6 79.4 reduce-scatter.1
where the time goes:
time: 685 us
  waiting for transfers between devices  245 us (36%)
  other arithmetic  225 us (33%)
  local copies, waits for them, and re-layouts  143 us (21%)
  matrix products  26.5 us (4%)
  blocking collectives  18.7 us (3%)
  between operations  13.2 us (2%)
  starting transfers between devices  12.8 us (2%)
    scatter-add x1, other arithmetic, scatter_rows(): target.at[flat_rows.reshape(-1)]  177 us
    gather x1, local copies, waits for them, and re-layouts, on_device(): picked = jnp.take(emb_table, flat_ids, axis=0, mode='fill', fill_value=0)  114 us
    all_to_all x1, waiting for transfers between devices, on_device(): lax.all_to_all(pooled_local, 'dp', split_axis=0, concat_axis=1, tiled=True)  87 us
    reduce_scatter x1, waiting for transfers between devices, on_device(): lax.psum_scatter(partial_value, 'fsdp', scatter_dimension=0, tiled=True)  79.6 us
    all_gather x1, waiting for transfers between devices, on_device(): lax.all_gather(cross_up, 'fsdp', axis=1, tiled=True)  48.7 us
    reduce_sum x1, other arithmetic, on_device(): jnp.sum(picked.astype(jnp.float32), axis=2).astype(jnp.bfloat16)  47.3 us
    all_to_all x1, waiting for transfers between devices, on_device(): lax.all_to_all(grad_pooled, 'dp', split_axis=1, concat_axis=0, tiled=True)  28.5 us
    all_to_all x1, blocking collectives, on_device(): lax.all_to_all(send_ids, 'dp', split_axis=1, concat_axis=0, tiled=True)  18.7 us
  transfers between devices with their start and end apart: 5, of which 4 were waited for; matrix products, arithmetic and copies ran while one was open for 26% of the time, Pallas kernels for 0%

commit v1 on v0

--- a/solution.py
+++ b/solution.py
@@ -2,6 +2,11 @@
 import jax.numpy as jnp
 from jax import lax
 from jax.sharding import PartitionSpec as P
+
+
+def exchange_gather(block, axis, along):
+    sent = jnp.stack([block] * lax.axis_size(axis))
+    return jnp.concatenate(lax.all_to_all(sent, axis, 0, 0), axis=along)
 
 
 def scatter_rows(height, index_rows, grads, table_count, slot_count, embed_width, offset):
@@ -38,7 +43,7 @@
     grad_gate = (upstream * pooled.astype(jnp.float32)).astype(jnp.bfloat16)
     down_full, up_full = (
         lax.all_gather(cross_down, "fsdp", axis=0, tiled=True),
-        lax.all_gather(cross_up, "fsdp", axis=1, tiled=True),
+        exchange_gather(cross_up, "fsdp", 1),
     )
     low_rank = jnp.dot(pooled, down_full, preferred_element_type=jnp.float32).astype(jnp.bfloat16)
     gate_value = jnp.dot(low_rank, up_full, preferred_element_type=jnp.float32) + cross_bias

time: 685 us -> 900 us (1.31)
  waiting for transfers between devices: 245 us -> 446 us
  local copies, waits for them, and re-layouts: 143 us -> 153 us
    all_to_all x0 -> x1, waiting for transfers between devices: none -> 287 us  [exchange_gather(): return jnp.concatenate(lax.all_to_all(sent, axis, 0, 0), axis=along)]
    all_to_all x1, waiting for transfers between devices: 87 us -> 25.2 us  [on_device(): lax.all_to_all(pooled_local, 'dp', split_axis=0, concat_axis=1, tiled=True)]
    all_gather x1 -> x0, waiting for transfers between devices: 48.7 us -> none  [on_device(): lax.all_gather(cross_up, 'fsdp', axis=1, tiled=True)]
    all_gather x1, waiting for transfers between devices: 0.01 us -> 24.1 us  [on_device(): lax.all_gather(cross_down, 'fsdp', axis=0, tiled=True)]
  transfers between devices with their start and end apart: 5 -> 5, of which waited for: 4 -> 5; matrix products, arithmetic and copies ran while one was open for 26% -> 1% of each run, Pallas kernels for 0% -> 0%
where the time goes in v1:
time: 900 us; the launch traced here: 899 us
  waiting for transfers between devices  446 us (50%)
  other arithmetic  226 us (25%)
  local copies, waits for them, and re-layouts  153 us (17%)
  matrix products  25.2 us (3%)
  blocking collectives  18.7 us (2%)
  starting transfers between devices  16.7 us (2%)
  between operations  13.5 us (2%)
    all_to_all x1, waiting for transfers between devices, exchange_gather(): return jnp.concatenate(lax.all_to_all(sent, axis, 0, 0), axis=along)  287 us
    scatter-add x1, other arithmetic, scatter_rows(): target.at[flat_rows.reshape(-1)]  177 us
    gather x1, local copies, waits for them, and re-layouts, on_device(): picked = jnp.take(emb_table, flat_ids, axis=0, mode='fill', fill_value=0)  115 us
    reduce_scatter x1, waiting for transfers between devices, on_device(): lax.psum_scatter(partial_value, 'fsdp', scatter_dimension=0, tiled=True)  80.3 us
    reduce_sum x1, other arithmetic, on_device(): jnp.sum(picked.astype(jnp.float32), axis=2).astype(jnp.bfloat16)  47.3 us
    all_to_all x1, waiting for transfers between devices, on_device(): lax.all_to_all(grad_pooled, 'dp', split_axis=1, concat_axis=0, tiled=True)  28.6 us
    all_to_all x1, waiting for transfers between devices, on_device(): lax.all_to_all(pooled_local, 'dp', split_axis=0, concat_axis=1, tiled=True)  25.2 us
    all_gather x1, waiting for transfers between devices, on_device(): lax.all_gather(cross_down, 'fsdp', axis=0, tiled=True)  24.1 us
  transfers between devices with their start and end apart: 5, of which 5 were waited for; matrix products, arithmetic and copies ran while one was open for 1% of the time, Pallas kernels for 0%

profile of v1, /device:TPU:1, one launch (start us, length us, event | category | flops | bytes accessed | tf_op | source)
XLA Modules:
  0.0 899.2 jit_solution(2645602364037097324)
XLA Ops:
  6.5 1.1 fusion.24
  7.6 18.7 %all_to_all.50 = s32[128,64,4]{0,2,1:T(4,128)S(1)} all-to-all(s32[128,64,4]{0,2,1:T(4,128)S(1)} %fusion.24), channel_id=1, replica_groups=mesh['dp'=64,'fsdp'=4] {'dp'}, dimensions={1} | all-to-all | bytes 262144 | tf_op jit(solution)/shard_map/all_to_all | solution.py:34
  26.4 2.6 copy.10
  29.0 4.9 reshape.193
  34.0 1.7 copy.9
  35.7 115.0 %gather_fusion = bf16[32768,128]{1,0:T(8,128)(2,1)} fusion(bf16[8192,128]{1,0:T(8,128)(2,1)S(1)} %copy-done, s32[32768]{0:T(1024)S(1)} %broadcast_clamp_fusion), kind=kCustom, calls=%fused_computation | custom fusion | bytes 16908288 | tf_op jit(solution)/shard_map/jit(_take)/gather | solution.py:38
  150.7 47.3 %select_reduce_fusion = bf16[8192,128]{1,0:T(8,128)(2,1)} fusion(bf16[8192,1,4,128]{3,2,0,1:T(4,128)(2,1)} %bitcast.57, pred[8192,4]{1,0:T(8,128)(4,1)S(1)} %copy.9), kind=kLoop, calls=%fused_computation.7 | loop fusion | flops 7340032 | bytes 10518528 | tf_op jit(solution)/shard_map/reduce_sum | solution.py:39
  198.0 4.5 all-to-all-start.1
  202.6 3.9 copy.12
  206.5 25.2 %all-to-all-done.1 = bf16[64,128,128]{2,1,0:T(8,128)(2,1)S(1)} async-done(((bf16[64,128,128]{2,1,0:T(8,128)(2,1)}), bf16[64,128,128]{2,1,0:T(8,128)(2,1)S(1)}, u32[]{:S(2)}, u32[]{:S(2)}) %all-to-all-start.1) | async-done | bytes 2097184 | tf_op jit(solution)/shard_map/all_to_all | solution.py:41
  231.7 5.5 stack.2
  237.2 7.3 all-to-all-start.2
  245.3 2.7 copy.8
  247.9 6.1 reshape.184
  254.0 287.0 %all-to-all-done.2 = bf16[4,512,2048]{1,2,0:T(8,128)(2,1)} async-done(((bf16[4,512,2048]{1,2,0:T(8,128)(2,1)}), bf16[4,512,2048]{1,2,0:T(8,128)(2,1)}, u32[]{:S(2)}, u32[]{:S(2)}) %all-to-all-start.2) | async-done | bytes 8388640 | tf_op jit(solution)/shard_map/all_to_all | solution.py:9
  541.0 24.1 %all-gather.2.cloned.1.call-done = bf16[8192,512]{1,0:T(8,128)(2,1)} async-done(((bf16[2048,512]{1,0:T(8,128)(2,1)}), bf16[8192,512]{1,0:T(8,128)(2,1)}) %all-gather.2.cloned.1.call-update) | async-done | bytes 8388624 | tf_op jit(solution)/shard_map/all_gather | solution.py:45
  565.1 12.3 %fusion.1 = f32[128,8192]{1,0:T(8,128)} fusion(bf16[512,8192]{0,1:T(8,128)(2,1)} %bitcast.10, bf16[128,8192]{1,0:T(8,128)(2,1)} %param.13, f32[8192]{0:T(1024)S(1)} %copy-done.2, bf16[8192,512]{1,0:T(8,128)(2,1)} %all-gather.2.cloned.1.call-done, bf16[64,128,128]{2,1,0:T(8,128)(2,1)S(1)} %all-to-all-done.1), kind=kOutput, calls=%fused_computation.5 | convolution fusion | flops 2151743488 | bytes 25198592 | tf_op jit(solution)/shard_map/dot_general | solution.py:49
  577.4 12.9 %fusion.13 = bf16[16,64,8,128]{3,2,1,0:T(8,128)(2,1)} fusion(f32[128,8192]{1,0:T(8,128)} %fusion.1, bf16[8192,512]{1,0:T(8,128)(2,1)} %all-gather.2.cloned.1.call-done, bf16[512,8192]{0,1:T(8,128)(2,1)} %bitcast.10, bf16[128,8192]{1,0:T(8,128)(2,1)} %param.13, bf16[64,128,128]{2,1,0:T(8,128)(2,1)S(1)} %all-to-all-done.1), kind=kOutput, calls=%fused_computation.19 | convolution fusion | flops 2153840640 | bytes 27262976 | tf_op jit(solution)/shard_map/dot_general | solution.py:53
  590.3 3.5 copy.33
  593.8 4.6 all-to-all-start.3
  598.9 28.6 %all-to-all-done.3 = bf16[128,64,128]{2,0,1:T(8,128)(2,1)S(1)} async-done(((bf16[128,64,128]{2,0,1:T(8,128)(2,1)}), bf16[128,64,128]{2,0,1:T(8,128)(2,1)S(1)}, u32[]{:S(2)}, u32[]{:S(2)}) %all-to-all-start.3) | async-done | bytes 2097184 | tf_op jit(solution)/shard_map/all_to_all | solution.py:57
  628.1 7.4 broadcast_in_dim.31
  635.5 176.5 %scatter_custom_fusion = f32[8192,128]{1,0:T(8,128)} fusion(s32[32768]{0:T(1024)S(1)} %bitcast.63, f32[32768,128]{1,0:T(8,128)} %bitcast.58, f32[]{:T(128)} %constant.7.clone.1), kind=kCustom, calls=%fused_computation.15 | custom fusion | flops 4194304 | bytes 4194816 | tf_op jit(solution)/shard_map/scatter-add | solution.py:21
  812.1 80.3 %reduce-scatter.2.cloned.1.call-done = f32[2048,128]{1,0:T(8,128)} async-done(((f32[8192,128]{1,0:T(8,128)}), f32[2048,128]{1,0:T(8,128)}) %reduce-scatter.2.cloned.1.call-update) | async-done | bytes 1048592 | tf_op jit(solution)/shard_map/reduce_scatter | solution.py:61
  (15 shorter events, 1.9 us)
Async XLA Ops:
  6.5 29.2 %copy-start = (bf16[8192,128]{1,0:T(8,128)(2,1)S(1)}, bf16[8192,128]{1,0:T(8,128)(2,1)}, u32[]{:S(2)}) copy-start(bf16[8192,128]{1,0:T(8,128)(2,1)} %param.9) | copy-start | bytes 6291460
  198.0 33.7 %all-to-all-start.1 = ((bf16[64,128,128]{2,1,0:T(8,128)(2,1)}), bf16[64,128,128]{2,1,0:T(8,128)(2,1)S(1)}, u32[]{:S(2)}, u32[]{:S(2)}) async-start(bf16[64,128,128]{2,1,0:T(8,128)(2,1)} %bitcast.61), calls=%async_computation.1 | async-start | bytes 4194304 | tf_op jit(solution)/shard_map/all_to_all | solution.py:41
  237.2 303.8 %all-to-all-start.2 = ((bf16[4,512,2048]{1,2,0:T(8,128)(2,1)}), bf16[4,512,2048]{1,2,0:T(8,128)(2,1)}, u32[]{:S(2)}, u32[]{:S(2)}) async-start(bf16[4,512,2048]{1,2,0:T(8,128)(2,1)} %stack.2), calls=%async_computation.2 | async-start | bytes 16777216 | tf_op jit(solution)/shard_map/all_to_all | solution.py:9
  244.5 320.6 %all-gather.2.cloned.1.call-start = ((), (), s32[]{:S(2)}) async-start(), calls=%async_computation.5 | async-start | bytes 10485760 | tf_op jit(solution)/shard_map/all_gather | solution.py:45
  245.2 319.9 %copy-start.2 = (f32[8192]{0:T(1024)S(1)}, f32[8192]{0:T(1024)}, u32[]{:S(2)}) copy-start(f32[8192]{0:T(1024)} %param.12) | copy-start | bytes 98308
  593.8 33.8 %all-to-all-start.3 = ((bf16[128,64,128]{2,0,1:T(8,128)(2,1)}), bf16[128,64,128]{2,0,1:T(8,128)(2,1)S(1)}, u32[]{:S(2)}, u32[]{:S(2)}) async-start(bf16[128,64,128]{2,0,1:T(8,128)(2,1)} %bitcast.60), calls=%async_computation.3 | async-start | bytes 4194304 | tf_op jit(solution)/shard_map/all_to_all | solution.py:57
  598.4 294.0 %reduce-scatter.2.cloned.1.call-start = ((), (), s32[]{:S(2)}) async-start(), calls=%async_computation.6 | async-start | bytes 5242880 | tf_op jit(solution)/shard_map/reduce_scatter | solution.py:61
  635.5 256.8 %copy-start.1 = (bf16[8192,128]{1,0:T(8,128)(2,1)S(1)}, bf16[8192,128]{1,0:T(8,128)(2,1)}, u32[]{:S(2)}) copy-start(bf16[8192,128]{1,0:T(8,128)(2,1)} %param.9) | copy-start | bytes 6291460
Sparse Core Ops, SparseCore 0:
  247.1 317.8 all-gather.1
  812.2 80.1 reduce-scatter.1
